TPU v7x, 128 devices: a whole 4x4x4 slice. The times are simulated.
128 devices in a mesh: det: 8 (over x, core), tm: 16 (over z, y).
Axes of the slice: x: 4, y: 4, z: 4, core: 2. Of those that a mesh axis runs over, the one named last changes fastest.
Arguments:
- samples: float32 [32, 1024, 128], P('det', 'tm'), may hold values from -6 to 6
- pointing: bfloat16 [32, 1024, 128, 128], P('det', 'tm'), may hold values from -0.25 to 0.25
- pix_block: int32 [32, 1024], P('det', 'tm'), may hold values from 0 to 8191, as said below
- det_weight: float32 [32], P('det'), may hold values from 0.5 to 2
- start_map: float32 [128, 8192], P(('det', 'tm')), may hold values from -6 to 6
- legendre: bfloat16 [1024, 6144, 128], P(('det', 'tm')), may hold values from -0.5 to 0.5
- prior_gain: float32 [6144], replicated, may hold values from 0.3 to 3
- m_values: int32 [1024], replicated, may hold values from 0 to 4095, as said below
- cycle_offset: int32 [128], P(('det', 'tm')), may hold values from 0 to 8191
Outputs:
- final_map: float32 [128, 8192], P(('det', 'tm'))
Inputs may be any that keep to these rules, and one draw needn't show every extreme that they name: `m_values`: strictly increasing; entry k lies in k * 4 to (k + 1) * 4 - 1, the first is 0 and the last is 4095. `pix_block`: the cycle owner of block b is the device holding cycle b // 64 of the map; among the 4 x 64 sample blocks of one device, at most 8 name blocks of any one owner, and on every device some owner gets exactly 8.
All inputs are finite; a program needn't handle non-finite values.
Results may differ from a plain program's by a relative error of at most 0.0042.
Values may be sent and summed in bfloat16 or wider, within the bound.
No kernel may reach another device: no remote copies, remote signals or barrier semaphores. Data moves between devices by JAX's collectives and lax.ppermute only.
A program may use at most 128 MiB of HBM per device.

v0:
```python
import math
import jax
import jax.numpy as jnp
from jax import lax
from jax.sharding import PartitionSpec as P

ITERS = 2
highest = lax.Precision.HIGHEST


def phase_pair(first_len, second_len, length, sign):
    first = jnp.arange(first_len, dtype=jnp.int32)[:, None]
    second = jnp.arange(second_len, dtype=jnp.int32)[None, :]
    phases = (first * second % length).astype(jnp.float32) * (sign * 2.0 * math.pi / length)
    return (jnp.cos(phases), jnp.sin(phases))


def forward_cycles(field):
    cycles, length = field.shape
    outer_len = length // 128
    shaped = field.reshape(cycles, outer_len, 128)
    cos_outer, sin_outer = phase_pair(outer_len, outer_len, outer_len, -1.0)
    part_re = jnp.einsum("mj,rjk->rmk", cos_outer, shaped, precision=highest)
    part_im = jnp.einsum("mj,rjk->rmk", sin_outer, shaped, precision=highest)
    cos_twist, sin_twist = phase_pair(outer_len, 128, length, -1.0)
    twist_re = part_re * cos_twist - part_im * sin_twist
    twist_im = part_re * sin_twist + part_im * cos_twist
    cos_inner, sin_inner = phase_pair(128, 128, 128, -1.0)
    spec_re = jnp.einsum("rmk,kn->rmn", twist_re, cos_inner, precision=highest) - jnp.einsum(
        "rmk,kn->rmn", twist_im, sin_inner, precision=highest
    )
    spec_im = jnp.einsum("rmk,kn->rmn", twist_re, sin_inner, precision=highest) + jnp.einsum(
        "rmk,kn->rmn", twist_im, cos_inner, precision=highest
    )
    return (spec_re.reshape(cycles, length), spec_im.reshape(cycles, length))


def inverse_cycles(spec_re, spec_im):
    cycles, length = spec_re.shape
    outer_len = length // 128
    shaped_re = spec_re.reshape(cycles, outer_len, 128)
    shaped_im = spec_im.reshape(cycles, outer_len, 128)
    cos_inner, sin_inner = phase_pair(128, 128, 128, 1.0)
    inner_re = jnp.einsum("rmn,nk->rmk", shaped_re, cos_inner, precision=highest) - jnp.einsum(
        "rmn,nk->rmk", shaped_im, sin_inner, precision=highest
    )
    inner_im = jnp.einsum("rmn,nk->rmk", shaped_re, sin_inner, precision=highest) + jnp.einsum(
        "rmn,nk->rmk", shaped_im, cos_inner, precision=highest
    )
    cos_twist, sin_twist = phase_pair(outer_len, 128, length, 1.0)
    twist_re = inner_re * cos_twist - inner_im * sin_twist
    twist_im = inner_re * sin_twist + inner_im * cos_twist
    cos_outer, sin_outer = phase_pair(outer_len, outer_len, outer_len, 1.0)
    field = jnp.einsum("jm,rmk->rjk", cos_outer, twist_re, precision=highest) - jnp.einsum(
        "jm,rmk->rjk", sin_outer, twist_im, precision=highest
    )
    return field.reshape(cycles, length)


def legendre_filter(owned, legendre, prior_gain, m_own):
    count_here, degrees, total_cycles = legendre.shape
    block_rows = min(512, degrees)

    def one_block(index, running):
        start = index * block_rows
        table = lax.dynamic_slice_in_dim(legendre, start, block_rows, 1)
        analysed = jnp.einsum("mlr,cmr->cml", table, owned, preferred_element_type=jnp.float32)
        degree = start + jnp.arange(block_rows, dtype=jnp.int32)
        keep_rows = degree[None, :] >= m_own[:, None]
        gain_block = lax.dynamic_slice_in_dim(prior_gain, start, block_rows)
        scaled = jnp.where(keep_rows[None], analysed * gain_block, 0.0).astype(jnp.bfloat16)
        return running + jnp.einsum(
            "mlr,cml->cmr", table, scaled, preferred_element_type=jnp.float32
        )

    first_block = 0
    initial = jnp.zeros(owned.shape, jnp.float32)
    summed = lax.fori_loop(first_block, degrees // block_rows, one_block, initial)
    return summed * math.sqrt(total_cycles / degrees)


def harmonic_filter(field, legendre, prior_gain, m_values, cycle_offset, m_own):
    cycles_here, length = field.shape
    count = m_values.shape[0]
    outer_len = length // 128
    spectrum_slot = m_values % outer_len * 128 + m_values // outer_len
    spec_re, spec_im = forward_cycles(field)
    pick_re = spec_re[:, spectrum_slot]
    pick_im = spec_im[:, spectrum_slot]
    phases = (m_values[None, :] * cycle_offset[:, None] % length).astype(jnp.float32) * (
        2.0 * math.pi / length
    )
    cos_phase = jnp.cos(phases)
    sin_phase = jnp.sin(phases)
    norm_factor = 1.0 / math.sqrt(length)
    coef_re = (pick_re * cos_phase + pick_im * sin_phase) * norm_factor
    coef_im = (pick_im * cos_phase - pick_re * sin_phase) * norm_factor
    outward = jnp.stack([coef_re.T, coef_im.T]).astype(jnp.bfloat16)
    owned = lax.all_to_all(outward, ("det", "tm"), split_axis=1, concat_axis=2, tiled=True)
    synth = legendre_filter(owned, legendre, prior_gain, m_own)
    returned = lax.all_to_all(synth, ("det", "tm"), split_axis=2, concat_axis=1, tiled=True)
    back_re = returned[0].T
    back_im = returned[1].T
    mode_weight = jnp.where(m_values == 0, 1.0, 2.0).astype(jnp.float32)[None, :]
    harm_re = mode_weight * (back_re * cos_phase - back_im * sin_phase)
    harm_im = mode_weight * (back_re * sin_phase + back_im * cos_phase)
    full_re = jnp.zeros((cycles_here, length), jnp.float32).at[:, spectrum_slot].set(harm_re)
    full_im = jnp.zeros((cycles_here, length), jnp.float32).at[:, spectrum_slot].set(harm_im)
    return inverse_cycles(full_re, full_im) / math.sqrt(2.0 * count)


def on_device(
    samples,
    pointing,
    pix_block,
    det_weight,
    start_map,
    legendre,
    prior_gain,
    m_values,
    cycle_offset,
):
    cycles_here, length = start_map.shape
    per_cycle = length // 128
    owners = lax.axis_size(("det", "tm"))
    total_cycles = cycles_here * owners
    nblocks = total_cycles * per_cycle
    count_here = legendre.shape[0]
    owner_index = lax.axis_index(("det", "tm"))
    m_own = lax.dynamic_slice_in_dim(m_values, owner_index * count_here, count_here)
    flat_pix = pix_block.reshape(-1)
    hit_terms = jnp.broadcast_to(det_weight[:, None], pix_block.shape).reshape(-1)
    hit_local = jnp.zeros((nblocks,), jnp.float32).at[flat_pix].add(hit_terms)
    hit_weight = lax.psum_scatter(
        hit_local.reshape(total_cycles, per_cycle), ("det", "tm"), scatter_dimension=0, tiled=True
    )
    divisor = jnp.repeat(1.0 + 0.25 * hit_weight, 128, axis=1)
    current = start_map
    for iteration in range(ITERS):
        map_half = current.astype(jnp.bfloat16)
        gathered = lax.all_gather(map_half, ("det", "tm"), axis=0, tiled=True).reshape(nblocks, 128)
        picked = gathered[pix_block]
        predicted = jnp.einsum(
            "dtsp,dtp->dts", pointing, picked, preferred_element_type=jnp.float32
        )
        weighted_resid = (det_weight[:, None, None] * (samples - predicted)).astype(jnp.bfloat16)
        binned_terms = jnp.einsum(
            "dtsp,dts->dtp", pointing, weighted_resid, preferred_element_type=jnp.float32
        )
        term_rows = binned_terms.reshape(-1, 128)
        local_map = jnp.zeros((nblocks, 128), jnp.float32).at[flat_pix].add(term_rows)
        local_map = local_map.reshape(total_cycles, length)
        binned = lax.psum_scatter(local_map, ("det", "tm"), scatter_dimension=0, tiled=True)
        filtered = harmonic_filter(current, legendre, prior_gain, m_values, cycle_offset, m_own)
        current = current + (binned - filtered) / divisor
    return current


def solution(mesh):
    placed = (
        P("det", "tm", None),
        P("det", "tm", None, None),
        P("det", "tm"),
        P("det"),
        P(("det", "tm"), None),
        P(("det", "tm"), None, None),
        P(),
        P(),
        P(("det", "tm")),
    )
    return jax.shard_map(
        on_device, mesh=mesh, in_specs=placed, out_specs=P(("det", "tm"), None), check_vma=False
    )
```

profile of v0, /device:TPU:1, one launch (start us, length us, event | category | flops | bytes accessed | tf_op | source)
XLA Modules:
  0.0 604.7 jit_solution(9442821672336099781)
XLA Ops:
  11.7 6.2 %gather_fusion.1 = f32[1024]{0:T(1024)S(1)} fusion(f32[8192]{0:T(1024)S(1)} %fusion.37, s32[1024]{0:T(1024)S(1)} %get-tuple-element.359), kind=kCustom, calls=%fused_computation.1 | custom fusion | bytes 12288 | tf_op jit(solution)/shard_map/gather | solution.py:88
  17.8 6.2 %gather_fusion.2 = f32[1024]{0:T(1024)S(1)} fusion(f32[8192]{0:T(1024)S(1)} %fusion.36, s32[1024]{0:T(1024)S(1)} %get-tuple-element.359), kind=kCustom, calls=%fused_computation.2 | custom fusion | bytes 12288 | tf_op jit(solution)/shard_map/gather | solution.py:89
  25.9 11.5 %all-to-all-start = ((bf16[2,1024,1]{2,0,1:T(2,128)(2,1)}), bf16[2,1024,1]{2,0,1:T(2,128)(2,1)S(1)}, u32[]{:S(2)}, u32[]{:S(2)}) async-start(bf16[2,1024,1]{2,0,1:T(2,128)(2,1)} %copy.46), calls=%async_computation | async-start | bytes 1048576 | tf_op jit(solution)/shard_map/all_to_all | solution.py:99
  40.6 68.5 %all-reduce.1 = f32[128,64]{1,0:T(8,128)S(1)} all-reduce(f32[128,64]{1,0:T(8,128)S(1)} %reshape.520), channel_id=3, replica_groups=mesh['det'=8,'tm'=16] {'det','tm'}, use_global_device_ids=true, to_apply=%region_7.8.clone | all-reduce | flops 8192 | bytes 65536
  109.8 35.5 %while.28 = (s32[]{:T(128)}, f32[2,8,128]{2,0,1:T(2,128)S(1)}, s32[8]{0:T(128)S(1)}, bf16[8,6144,128]{2,1,0:T(8,128)(2,1)}, bf16[2,8,128]{2,0,1:T(2,128)(2,1)S(1...) while((s32[]{:T(128)}, f32[2,8,128]{2,0,1:T(2,128)S(1)}, ...), condition=%wide.region_3.0_spmd.clone, body=%wide.region_2.0_spmd.clone.sunk | while | flops 4227591 | bytes 2137796 | solution.py:78
  110.6 2.1 fusion.350
  119.5 2.1 fusion.350
  128.3 2.2 fusion.350
  134.3 2.1 fusion.350
  137.3 2.1 fusion.350
  140.2 2.1 fusion.350
  145.3 12.6 %reduce = bf16[128,8192]{1,0:T(8,128)(2,1)S(1)} reduce(bf16[128,1,8192]{2,1,0:T(2,128)(2,1)} %all-gather.5.cloned.1.call-done, bf16[]{:T(256)} %constant.249), dimensions={1}, to_apply=%all-gather.reduce_sub_computation | reduce | bytes 4194306 | tf_op jit(solution)/shard_map/all_gather | solution.py:141
  157.9 2.4 reshape.509
  160.3 2.6 gather_fusion
  162.9 7.8 %fusion.44 = f32[4,64,1,128]{3,2,1,0:T(1,128)S(1)} fusion(bf16[4,64,128,128]{3,2,1,0:T(8,128)(2,1)} %param.14, bf16[4,64,128,1]{2,1,0,3:T(8,128)(2,1)S(1)} %bitcast.179), kind=kOutput, calls=%fused_computation.73 | convolution fusion | flops 8388608 | bytes 8585216 | tf_op jit(solution)/shard_map/dtsp,dtp->dts/dot_general | solution.py:143
  170.8 5.7 fusion.42
  176.5 3.6 scatter_custom_fusion
  180.1 4.9 reshape.511
  185.8 4.7 all-to-all-start.1
  190.7 10.1 %all-to-all-done.1 = f32[2,8,128]{1,0,2:T(2,128)S(1)} async-done(((f32[2,8,128]{1,0,2:T(2,128)}), f32[2,8,128]{1,0,2:T(2,128)S(1)}, u32[]{:S(2)}, u32[]{:S(2)}) %all-to-all-start.1) | async-done | bytes 8224 | tf_op jit(solution)/shard_map/all_to_all | solution.py:101
  201.5 4.5 scatter_custom_fusion.1
  206.0 4.3 scatter_custom_fusion.2
  213.0 123.0 %all-reduce.6.cloned.1.call-done = f32[128,8192]{1,0:T(8,128)} async-done(((f32[128,8192]{1,0:T(8,128)}), f32[128,8192]{1,0:T(8,128)}) %all-reduce.6.cloned.1.call-update) | async-done | bytes 4194320
  339.5 6.2 %gather_fusion.4 = f32[1024]{0:T(1024)S(1)} fusion(f32[8192]{0:T(1024)S(1)} %fusion.34, s32[1024]{0:T(1024)S(1)} %get-tuple-element.359), kind=kCustom, calls=%fused_computation.4 | custom fusion | bytes 12288 | tf_op jit(solution)/shard_map/gather | solution.py:88
  346.8 6.2 %gather_fusion.5 = f32[1024]{0:T(1024)S(1)} fusion(f32[8192]{0:T(1024)S(1)} %fusion.33, s32[1024]{0:T(1024)S(1)} %get-tuple-element.359), kind=kCustom, calls=%fused_computation.5 | custom fusion | bytes 12288 | tf_op jit(solution)/shard_map/gather | solution.py:89
  354.2 6.6 %all-to-all-start.2 = ((bf16[2,1024,1]{2,0,1:T(2,128)(2,1)}), bf16[2,1024,1]{2,0,1:T(2,128)(2,1)S(1)}, u32[]{:S(2)}, u32[]{:S(2)}) async-start(bf16[2,1024,1]{2,0,1:T(2,128)(2,1)} %copy.51), calls=%async_computation.2 | async-start | bytes 1048576 | tf_op jit(solution)/shard_map/all_to_all | solution.py:99
  361.0 13.8 %all-to-all-done.2 = bf16[2,1024,1]{2,0,1:T(2,128)(2,1)S(1)} async-done(((bf16[2,1024,1]{2,0,1:T(2,128)(2,1)}), bf16[2,1024,1]{2,0,1:T(2,128)(2,1)S(1)}, u32[]{:S(2)}, u32[]{:S(2)}) %all-to-all-start.2) | async-done | bytes 4128 | tf_op jit(solution)/shard_map/all_to_all | solution.py:99
  375.4 29.4 %all-gather.7.cloned.1.call-done = bf16[128,1,8192]{2,1,0:T(2,128)(2,1)} async-done(((bf16[1,1,8192]{2,1,0:T(2,128)(2,1)}), bf16[128,1,8192]{2,1,0:T(2,128)(2,1)}) %all-gather.7.cloned.1.call-update) | async-done | bytes 2097168 | tf_op jit(solution)/shard_map/all_gather | solution.py:141
  404.9 12.6 %reduce.3 = bf16[128,8192]{1,0:T(8,128)(2,1)S(1)} reduce(bf16[128,1,8192]{2,1,0:T(2,128)(2,1)} %all-gather.7.cloned.1.call-done, bf16[]{:T(256)} %constant.249), dimensions={1}, to_apply=%all-gather.1.reduce_sub_computation | reduce | bytes 4194306 | tf_op jit(solution)/shard_map/all_gather | solution.py:141
  417.5 2.4 reshape.521
  419.8 2.6 gather_fusion.3
  422.4 7.8 %fusion.40 = f32[4,64,1,128]{3,2,1,0:T(1,128)S(1)} fusion(bf16[4,64,128,128]{3,2,1,0:T(8,128)(2,1)} %param.14, bf16[4,64,128,1]{2,1,0,3:T(8,128)(2,1)S(1)} %bitcast.178), kind=kOutput, calls=%fused_computation.69 | convolution fusion | flops 8388608 | bytes 8585216 | tf_op jit(solution)/shard_map/dtsp,dtp->dts/dot_general | solution.py:143
  430.3 5.7 fusion.38
  436.0 3.6 scatter_custom_fusion.4
  439.6 4.9 reshape.523
  444.6 35.7 %while.29 = (s32[]{:T(128)}, f32[2,8,128]{2,0,1:T(2,128)S(1)}, s32[8]{0:T(128)S(1)}, bf16[8,6144,128]{2,1,0:T(8,128)(2,1)}, bf16[2,8,128]{2,0,1:T(2,128)(2,1)S(1...) while((s32[]{:T(128)}, f32[2,8,128]{2,0,1:T(2,128)S(1)}, ...), condition=%wide.region_11.12_spmd.clone, body=%wide.region_10.11_spmd.clone.sunk | while | flops 4227591 | bytes 2137796 | solution.py:78
  445.4 2.1 fusion.354
  454.3 2.1 fusion.354
  460.2 2.1 fusion.354
  463.2 2.2 fusion.354
  466.2 2.1 fusion.354
  469.2 2.1 fusion.354
  472.2 2.1 fusion.354
  475.2 2.1 fusion.354
  480.4 15.8 %all_to_all.66 = f32[2,8,128]{1,0,2:T(2,128)S(1)} all-to-all(f32[2,8,128]{1,0,2:T(2,128)S(1)} %copy.55), channel_id=1, replica_groups=mesh['det'=8,'tm'=16] {'det','tm'}, dimensions={2} | all-to-all | bytes 16384 | tf_op jit(solution)/shard_map/all_to_all | solution.py:101
  496.8 4.3 scatter_custom_fusion.5
  501.2 4.3 scatter_custom_fusion.6
  508.1 88.1 %all-reduce.8.cloned.1.call-done = f32[128,8192]{1,0:T(8,128)} async-done(((f32[128,8192]{1,0:T(8,128)}), f32[128,8192]{1,0:T(8,128)}) %all-reduce.8.cloned.1.call-update) | async-done | bytes 4194320
  (175 shorter events, 66.9 us)
Async XLA Ops:
  11.6 13.0 %copy-start.1 = (s32[1024]{0:T(1024)S(1)}, s32[1024]{0:T(1024)}, u32[]{:S(2)}) copy-start(s32[1024]{0:T(1024)} %param.20) | copy-start | bytes 12292
  11.6 25.8 %copy-start.2 = (f32[1,8192]{1,0:T(1,128)S(1)}, f32[1,8192]{1,0:T(1,128)}, u32[]{:S(2)}) copy-start(f32[1,8192]{1,0:T(1,128)} %param.17) | copy-start | bytes 98308
  11.7 26.6 %copy-start.3 = (s32[4,64]{1,0:T(4,128)S(1)}, s32[4,64]{1,0:T(4,128)}, u32[]{:S(2)}) copy-start(s32[4,64]{1,0:T(4,128)} %param.15) | copy-start | bytes 3076
  11.7 26.7 %copy-start.4 = (f32[4]{0:T(128)S(1)}, f32[4]{0:T(128)}, u32[]{:S(2)}) copy-start(f32[4]{0:T(128)} %param.16) | copy-start | bytes 52
  25.9 83.3 %all-to-all-start = ((bf16[2,1024,1]{2,0,1:T(2,128)(2,1)}), bf16[2,1024,1]{2,0,1:T(2,128)(2,1)S(1)}, u32[]{:S(2)}, u32[]{:S(2)}) async-start(bf16[2,1024,1]{2,0,1:T(2,128)(2,1)} %copy.46), calls=%async_computation | async-start | bytes 1048576 | tf_op jit(solution)/shard_map/all_to_all | solution.py:99
  37.4 107.9 %all-gather.5.cloned.1.call-start = ((), (), s32[]{:S(2)}) async-start(), calls=%async_computation.4 | async-start | bytes 4227072 | tf_op jit(solution)/shard_map/all_gather | solution.py:141
  38.2 297.8 %all-reduce.6.cloned.1.call-start = ((), (), s32[]{:S(2)}) async-start(), calls=%async_computation.6 | async-start | bytes 8388608
  162.9 7.8 %copy-start = (f32[4,64,128]{2,1,0:T(8,128)S(1)}, f32[4,64,128]{2,1,0:T(8,128)}, u32[]{:S(2)}) copy-start(f32[4,64,128]{2,1,0:T(8,128)} %param.13) | copy-start | bytes 393220
  185.8 15.0 %all-to-all-start.1 = ((f32[2,8,128]{1,0,2:T(2,128)}), f32[2,8,128]{1,0,2:T(2,128)S(1)}, u32[]{:S(2)}, u32[]{:S(2)}) async-start(f32[2,8,128]{1,0,2:T(2,128)} %copy.50), calls=%async_computation.1 | async-start | bytes 262144 | tf_op jit(solution)/shard_map/all_to_all | solution.py:101
  190.6 214.3 %all-gather.7.cloned.1.call-start = ((), (), s32[]{:S(2)}) async-start(), calls=%async_computation.5 | async-start | bytes 4227072 | tf_op jit(solution)/shard_map/all_gather | solution.py:141
  354.2 20.6 %all-to-all-start.2 = ((bf16[2,1024,1]{2,0,1:T(2,128)(2,1)}), bf16[2,1024,1]{2,0,1:T(2,128)(2,1)S(1)}, u32[]{:S(2)}, u32[]{:S(2)}) async-start(bf16[2,1024,1]{2,0,1:T(2,128)(2,1)} %copy.51), calls=%async_computation.2 | async-start | bytes 1048576 | tf_op jit(solution)/shard_map/all_to_all | solution.py:99
  360.8 235.5 %all-reduce.8.cloned.1.call-start = ((), (), s32[]{:S(2)}) async-start(), calls=%async_computation.7 | async-start | bytes 8388608
Sparse Core Ops, SparseCore 0:
  41.4 68.8 all-gather.4
  185.2 150.7 all-reduce.5
  339.2 65.6 all-gather.6
  444.7 151.5 all-reduce.7
where the time goes:
time: 611 us; the launch traced here: 605 us
  waiting for transfers between devices  265 us (43%)
  matrix products  89.6 us (15%)
  local copies, waits for them, and re-layouts  86.5 us (14%)
  blocking collectives  84.3 us (14%)
  other arithmetic  41.5 us (7%)
  starting transfers between devices  23.2 us (4%)
  between operations  14.5 us (2%)
    unnamed x6, waiting for transfers between devices  211 us
    unnamed x1, blocking collectives  68.5 us
    dot_general x24, matrix products, one_block(): jnp.einsum('mlr,cml->cmr', table, scaled, preferred_element_type=jnp.floa...  50.4 us
    all_gather x2, waiting for transfers between devices, on_device(): lax.all_gather(map_half, ('det', 'tm'), axis=0, tiled=True)  29.4 us
    all_gather x2, other arithmetic, on_device(): lax.all_gather(map_half, ('det', 'tm'), axis=0, tiled=True)  25.2 us
    dynamic_slice x24, local copies, waits for them, and re-layouts, one_block(): gain_block = lax.dynamic_slice_in_dim(prior_gain, start, block_rows)  18.3 us
    all_to_all x2, starting transfers between devices, harmonic_filter(): lax.all_to_all(outward, ('det', 'tm'), split_axis=1, concat_axis=2, tiled...  18.1 us
    scatter x4, local copies, waits for them, and re-layouts, harmonic_filter(): jnp.zeros((cycles_here, length), jnp.float32).at[:, spectrum_slot]  17.6 us
  transfers between devices with their start and end apart: 7, of which 5 were waited for; matrix products, arithmetic and copies ran while one was open for 19% of the time, Pallas kernels for 0%

commit v1 on v0

--- a/solution.py
+++ b/solution.py
@@ -138,7 +138,12 @@
     current = start_map
     for iteration in range(ITERS):
         map_half = current.astype(jnp.bfloat16)
-        gathered = lax.all_gather(map_half, ("det", "tm"), axis=0, tiled=True).reshape(nblocks, 128)
+        gathered = jnp.concatenate(
+            lax.all_to_all(
+                jnp.stack([map_half] * lax.axis_size(("det", "tm"))), ("det", "tm"), 0, 0
+            ),
+            axis=0,
+        ).reshape(nblocks, 128)
         picked = gathered[pix_block]
         predicted = jnp.einsum(
             "dtsp,dtp->dts", pointing, picked, preferred_element_type=jnp.float32

time: 611 us -> 676 us (1.11)
  local copies, waits for them, and re-layouts: 86.5 us -> 119 us
  other arithmetic: 41.5 us -> 66.8 us
  starting transfers between devices: 23.2 us -> 42.4 us
  waiting for transfers between devices: 265 us -> 250 us
    all_gather x2 -> x0, waiting for transfers between devices: 29.4 us -> none  [on_device(): lax.all_gather(map_half, ('det', 'tm'), axis=0, tiled=True)]
    all_to_all x0 -> x2, waiting for transfers between devices: none -> 28.6 us  [on_device(): lax.all_to_all(jnp.stack([map_half] * lax.axis_size(('det', 'tm'))), ('de...]
    another operation x2 -> x4, other arithmetic: 0.11 us -> 26.5 us  [the longest x2 26.4 us: on_device(): jnp.stack([map_half] * lax.axis_size(('det', 'tm')))]
    all_gather x2 -> x0, other arithmetic: 25.2 us -> none  [on_device(): lax.all_gather(map_half, ('det', 'tm'), axis=0, tiled=True)]
    all_to_all x0 -> x2, other arithmetic: none -> 25.2 us  [on_device(): lax.all_to_all(jnp.stack([map_half] * lax.axis_size(('det', 'tm'))), ('de...]
    unnamed x12 -> x16, local copies, waits for them, and re-layouts: 0.21 us -> 19.3 us
    another operation x0 -> x5, local copies, waits for them, and re-layouts: none -> 17.5 us  [the longest x3 12.8 us: on_device(): jnp.stack([map_half] * lax.axis_size(('det', 'tm')))]
    all_to_all x0 -> x2, starting transfers between devices: none -> 14.5 us  [on_device(): lax.all_to_all(jnp.stack([map_half] * lax.axis_size(('det', 'tm'))), ('de...]
  transfers between devices with their start and end apart: 7 -> 7, of which waited for: 5 -> 4; matrix products, arithmetic and copies ran while one was open for 19% -> 22% of each run, Pallas kernels for 0% -> 0%
where the time goes in v1:
time: 676 us; the launch traced here: 665 us
  waiting for transfers between devices  250 us (37%)
  local copies, waits for them, and re-layouts  119 us (18%)
  matrix products  89.6 us (13%)
  blocking collectives  83.2 us (12%)
  other arithmetic  66.8 us (10%)
  starting transfers between devices  42.4 us (6%)
  between operations  14.8 us (2%)
    unnamed x4, waiting for transfers between devices  211 us
    unnamed x1, blocking collectives  67.4 us
    dot_general x24, matrix products, one_block(): jnp.einsum('mlr,cml->cmr', table, scaled, preferred_element_type=jnp.floa...  50.4 us
    all_to_all x2, waiting for transfers between devices, on_device(): lax.all_to_all(jnp.stack([map_half] * lax.axis_size(('det', 'tm'))), ('de...  28.6 us
    another operation x2, other arithmetic, on_device(): jnp.stack([map_half] * lax.axis_size(('det', 'tm')))  26.4 us
    all_to_all x2, other arithmetic, on_device(): lax.all_to_all(jnp.stack([map_half] * lax.axis_size(('det', 'tm'))), ('de...  25.2 us
    unnamed x16, local copies, waits for them, and re-layouts  19.3 us
    dynamic_slice x24, local copies, waits for them, and re-layouts, one_block(): gain_block = lax.dynamic_slice_in_dim(prior_gain, start, block_rows)  18.4 us
  transfers between devices with their start and end apart: 7, of which 4 were waited for; matrix products, arithmetic and copies ran while one was open for 22% of the time, Pallas kernels for 0%

profile of v1, /device:TPU:1, one launch (start us, length us, event | category | flops | bytes accessed | tf_op | source)
XLA Modules:
  0.0 665.5 jit_solution(4751317596054363744)
XLA Ops:
  11.7 6.2 gather_fusion.1
  17.8 6.2 gather_fusion.2
  25.9 11.5 %all-to-all-start.1 = ((bf16[2,1024,1]{2,0,1:T(2,128)(2,1)}), bf16[2,1024,1]{2,0,1:T(2,128)(2,1)S(1)}, u32[]{:S(2)}, u32[]{:S(2)}) async-start(bf16[2,1024,1]{2,0,1:T(2,128)(2,1)} %copy.46), calls=%async_computation.1 | async-start | bytes 1048576 | tf_op jit(solution)/shard_map/all_to_all | solution.py:99
  39.9 67.4 %all-reduce.1 = f32[128,64]{1,0:T(8,128)S(1)} all-reduce(f32[128,64]{1,0:T(8,128)S(1)} %reshape.519), channel_id=3, replica_groups=mesh['det'=8,'tm'=16] {'det','tm'}, use_global_device_ids=true, to_apply=%region_7.8.clone | all-reduce | flops 8192 | bytes 65536
  107.4 6.1 stack.16
  114.1 13.2 %reduce.22 = bf16[128,8192]{1,0:T(8,128)(2,1)S(1)} reduce(bf16[128,1,8192]{2,1,0:T(2,128)(2,1)} %stack.16, bf16[]{:T(256)} %broadcast.847), dimensions={1}, to_apply=%stack.16.reduce_sub_computation | reduce | bytes 4194306 | tf_op jit(solution)/shard_map/stack | solution.py:143
  127.3 2.8 reshape.725
  130.1 4.7 all-to-all-start
  135.5 35.5 %while.28 = (s32[]{:T(128)}, f32[2,8,128]{2,0,1:T(2,128)S(1)}, s32[8]{0:T(128)S(1)}, bf16[8,6144,128]{2,1,0:T(8,128)(2,1)}, bf16[2,8,128]{2,0,1:T(2,128)(2,1)S(1...) while((s32[]{:T(128)}, f32[2,8,128]{2,0,1:T(2,128)S(1)}, ...), condition=%wide.region_3.0_spmd.clone, body=%wide.region_2.0_spmd.clone.sunk | while | flops 4227591 | bytes 2137796 | solution.py:78
  136.3 2.1 fusion.350
  145.2 2.1 fusion.350
  154.0 2.2 fusion.350
  171.0 6.8 %reshape.726 = bf16[128,1,8192]{2,1,0:T(2,128)(2,1)} reshape(bf16[128,2,4096]{2,1,0:T(2,128)(2,1)S(1)} %all-to-all-done) | data formatting | bytes 4194304
  177.8 12.6 %reduce.1 = bf16[128,8192]{1,0:T(8,128)(2,1)S(1)} reduce(bf16[128,1,8192]{2,1,0:T(2,128)(2,1)} %reshape.726, bf16[]{:T(256)} %constant.249), dimensions={1}, to_apply=%all_to_all.54.reduce_sub_computation | reduce | bytes 4194306 | tf_op jit(solution)/shard_map/all_to_all | solution.py:142
  190.4 2.4 reshape_reshape.6
  192.7 2.6 gather_fusion
  195.3 7.8 %fusion.44 = f32[4,64,1,128]{3,2,1,0:T(1,128)S(1)} fusion(bf16[4,64,128,128]{3,2,1,0:T(8,128)(2,1)} %param.14, bf16[4,64,128,1]{2,1,0,3:T(8,128)(2,1)S(1)} %bitcast.175), kind=kOutput, calls=%fused_computation.73 | convolution fusion | flops 8388608 | bytes 8585216 | tf_op jit(solution)/shard_map/dtsp,dtp->dts/dot_general | solution.py:148
  203.3 5.7 fusion.42
  208.9 3.6 scatter_custom_fusion
  212.6 4.9 reshape.510
  218.3 9.8 %all-to-all-start.2 = ((f32[2,8,128]{1,0,2:T(2,128)}), f32[2,8,128]{1,0,2:T(2,128)S(1)}, u32[]{:S(2)}, u32[]{:S(2)}) async-start(f32[2,8,128]{1,0,2:T(2,128)} %copy.50), calls=%async_computation.2 | async-start | bytes 262144 | tf_op jit(solution)/shard_map/all_to_all | solution.py:101
  228.1 10.2 %all-to-all-done.2 = f32[2,8,128]{1,0,2:T(2,128)S(1)} async-done(((f32[2,8,128]{1,0,2:T(2,128)}), f32[2,8,128]{1,0,2:T(2,128)S(1)}, u32[]{:S(2)}, u32[]{:S(2)}) %all-to-all-start.2) | async-done | bytes 8224 | tf_op jit(solution)/shard_map/all_to_all | solution.py:101
  239.0 4.6 scatter_custom_fusion.1
  243.5 4.3 scatter_custom_fusion.2
  250.5 123.0 %all-reduce.6.cloned.1.call-done = f32[128,8192]{1,0:T(8,128)} async-done(((f32[128,8192]{1,0:T(8,128)}), f32[128,8192]{1,0:T(8,128)}) %all-reduce.6.cloned.1.call-update) | async-done | bytes 4194320
  376.9 6.2 gather_fusion.4
  383.7 6.2 gather_fusion.5
  391.1 6.6 all-to-all-start.4
  397.7 6.1 stack.20
  403.8 13.2 %reduce.23 = bf16[128,8192]{1,0:T(8,128)(2,1)S(1)} reduce(bf16[128,1,8192]{2,1,0:T(2,128)(2,1)} %stack.20, bf16[]{:T(256)} %broadcast.847), dimensions={1}, to_apply=%stack.20.reduce_sub_computation | reduce | bytes 4194306 | tf_op jit(solution)/shard_map/stack | solution.py:143
  417.0 2.8 reshape.727
  419.8 9.8 %all-to-all-start.3 = ((bf16[128,2,4096]{2,1,0:T(2,128)(2,1)}), bf16[128,2,4096]{2,1,0:T(2,128)(2,1)S(1)}, u32[]{:S(2)}, u32[]{:S(2)}) async-start(bf16[128,2,4096]{2,1,0:T(2,128)(2,1)} %reshape.727), calls=%async_computation.3 | async-start | bytes 4194304 | tf_op jit(solution)/shard_map/all_to_all | solution.py:142
  430.2 28.6 %all-to-all-done.3 = bf16[128,2,4096]{2,1,0:T(2,128)(2,1)S(1)} async-done(((bf16[128,2,4096]{2,1,0:T(2,128)(2,1)}), bf16[128,2,4096]{2,1,0:T(2,128)(2,1)S(1)}, u32[]{:S(2)}, u32[]{:S(2)}) %all-to-all-start.3) | async-done | bytes 2097184 | tf_op jit(solution)/shard_map/all_to_all | solution.py:142
  458.8 6.8 %reshape.728 = bf16[128,1,8192]{2,1,0:T(2,128)(2,1)} reshape(bf16[128,2,4096]{2,1,0:T(2,128)(2,1)S(1)} %all-to-all-done.3) | data formatting | bytes 4194304
  465.6 12.6 %reduce.5 = bf16[128,8192]{1,0:T(8,128)(2,1)S(1)} reduce(bf16[128,1,8192]{2,1,0:T(2,128)(2,1)} %reshape.728, bf16[]{:T(256)} %constant.249), dimensions={1}, to_apply=%all_to_all.62.reduce_sub_computation | reduce | bytes 4194306 | tf_op jit(solution)/shard_map/all_to_all | solution.py:142
  478.2 2.4 reshape_reshape.7
  480.6 2.6 gather_fusion.3
  483.2 7.8 %fusion.40 = f32[4,64,1,128]{3,2,1,0:T(1,128)S(1)} fusion(bf16[4,64,128,128]{3,2,1,0:T(8,128)(2,1)} %param.14, bf16[4,64,128,1]{2,1,0,3:T(8,128)(2,1)S(1)} %bitcast.174), kind=kOutput, calls=%fused_computation.69 | convolution fusion | flops 8388608 | bytes 8585216 | tf_op jit(solution)/shard_map/dtsp,dtp->dts/dot_general | solution.py:148
  491.1 5.7 fusion.38
  496.7 3.6 scatter_custom_fusion.4
  500.3 4.9 reshape.521
  505.3 35.7 %while.29 = (s32[]{:T(128)}, f32[2,8,128]{2,0,1:T(2,128)S(1)}, s32[8]{0:T(128)S(1)}, bf16[8,6144,128]{2,1,0:T(8,128)(2,1)}, bf16[2,8,128]{2,0,1:T(2,128)(2,1)S(1...) while((s32[]{:T(128)}, f32[2,8,128]{2,0,1:T(2,128)S(1)}, ...), condition=%wide.region_11.12_spmd.clone, body=%wide.region_10.11_spmd.clone.sunk | while | flops 4227591 | bytes 2137796 | solution.py:78
  506.2 2.1 fusion.354
  524.0 2.2 fusion.354
  541.2 15.7 %all_to_all.76 = f32[2,8,128]{1,0,2:T(2,128)S(1)} all-to-all(f32[2,8,128]{1,0,2:T(2,128)S(1)} %copy.55), channel_id=1, replica_groups=mesh['det'=8,'tm'=16] {'det','tm'}, dimensions={2} | all-to-all | bytes 16384 | tf_op jit(solution)/shard_map/all_to_all | solution.py:101
  557.5 4.5 scatter_custom_fusion.5
  562.1 4.3 scatter_custom_fusion.6
  569.0 87.8 %all-reduce.8.cloned.1.call-done = f32[128,8192]{1,0:T(8,128)} async-done(((f32[128,8192]{1,0:T(8,128)}), f32[128,8192]{1,0:T(8,128)}) %all-reduce.8.cloned.1.call-update) | async-done | bytes 4194320
  (182 shorter events, 85.1 us)
Async XLA Ops:
  11.6 13.0 %copy-start.1 = (s32[1024]{0:T(1024)S(1)}, s32[1024]{0:T(1024)}, u32[]{:S(2)}) copy-start(s32[1024]{0:T(1024)} %param.20) | copy-start | bytes 12292
  11.6 25.8 %copy-start.2 = (f32[1,8192]{1,0:T(1,128)S(1)}, f32[1,8192]{1,0:T(1,128)}, u32[]{:S(2)}) copy-start(f32[1,8192]{1,0:T(1,128)} %param.17) | copy-start | bytes 98308
  11.7 25.9 %copy-start.3 = (s32[4,64]{1,0:T(4,128)S(1)}, s32[4,64]{1,0:T(4,128)}, u32[]{:S(2)}) copy-start(s32[4,64]{1,0:T(4,128)} %param.15) | copy-start | bytes 3076
  11.7 26.0 %copy-start.4 = (f32[4]{0:T(128)S(1)}, f32[4]{0:T(128)}, u32[]{:S(2)}) copy-start(f32[4]{0:T(128)} %param.16) | copy-start | bytes 52
  25.9 104.2 %all-to-all-start.1 = ((bf16[2,1024,1]{2,0,1:T(2,128)(2,1)}), bf16[2,1024,1]{2,0,1:T(2,128)(2,1)S(1)}, u32[]{:S(2)}, u32[]{:S(2)}) async-start(bf16[2,1024,1]{2,0,1:T(2,128)(2,1)} %copy.46), calls=%async_computation.1 | async-start | bytes 1048576 | tf_op jit(solution)/shard_map/all_to_all | solution.py:99
  130.1 40.9 %all-to-all-start = ((bf16[128,2,4096]{2,1,0:T(2,128)(2,1)}), bf16[128,2,4096]{2,1,0:T(2,128)(2,1)S(1)}, u32[]{:S(2)}, u32[]{:S(2)}) async-start(bf16[128,2,4096]{2,1,0:T(2,128)(2,1)} %reshape.725), calls=%async_computation | async-start | bytes 4194304 | tf_op jit(solution)/shard_map/all_to_all | solution.py:142
  134.8 238.6 %all-reduce.6.cloned.1.call-start = ((), (), s32[]{:S(2)}) async-start(), calls=%async_computation.6 | async-start | bytes 8388608
  195.3 7.8 %copy-start = (f32[4,64,128]{2,1,0:T(8,128)S(1)}, f32[4,64,128]{2,1,0:T(8,128)}, u32[]{:S(2)}) copy-start(f32[4,64,128]{2,1,0:T(8,128)} %param.13) | copy-start | bytes 393220
  218.3 20.0 %all-to-all-start.2 = ((f32[2,8,128]{1,0,2:T(2,128)}), f32[2,8,128]{1,0,2:T(2,128)S(1)}, u32[]{:S(2)}, u32[]{:S(2)}) async-start(f32[2,8,128]{1,0,2:T(2,128)} %copy.50), calls=%async_computation.2 | async-start | bytes 262144 | tf_op jit(solution)/shard_map/all_to_all | solution.py:101
  391.1 28.7 %all-to-all-start.4 = ((bf16[2,1024,1]{2,0,1:T(2,128)(2,1)}), bf16[2,1024,1]{2,0,1:T(2,128)(2,1)S(1)}, u32[]{:S(2)}, u32[]{:S(2)}) async-start(bf16[2,1024,1]{2,0,1:T(2,128)(2,1)} %copy.51), calls=%async_computation.4 | async-start | bytes 1048576 | tf_op jit(solution)/shard_map/all_to_all | solution.py:99
  419.8 39.0 %all-to-all-start.3 = ((bf16[128,2,4096]{2,1,0:T(2,128)(2,1)}), bf16[128,2,4096]{2,1,0:T(2,128)(2,1)S(1)}, u32[]{:S(2)}, u32[]{:S(2)}) async-start(bf16[128,2,4096]{2,1,0:T(2,128)(2,1)} %reshape.727), calls=%async_computation.3 | async-start | bytes 4194304 | tf_op jit(solution)/shard_map/all_to_all | solution.py:142
  429.6 227.2 %all-reduce.8.cloned.1.call-start = ((), (), s32[]{:S(2)}) async-start(), calls=%async_computation.7 | async-start | bytes 8388608
Sparse Core Ops, SparseCore 0:
  217.6 155.7 all-reduce.5
  505.4 151.3 all-reduce.7
